TPU v7x, 32 devices: a whole 2x2x4 slice. The times are simulated.
32 devices in a mesh: req: 4 (over x, core), tok: 8 (over z, y).
Axes of the slice: x: 2, y: 2, z: 4, core: 2. Of those that a mesh axis runs over, the one named last changes fastest.
Arguments:
- queries: bfloat16 [8, 2048, 2048], P('req', 'tok'), may hold values from -16 to 16
- new_kv: bfloat16 [8, 2048, 256], P('req', 'tok'), may hold values from -6 to 6
- cache_kv: bfloat16 [8, 4096, 256], P('req', 'tok'), may hold values from -6 to 6
- residual: bfloat16 [8, 2048, 2048], P('req', 'tok'), may hold values from -24 to 24
- prefix_len: int32 [8], replicated, may hold values from 0 to 4096, as said below
- dest_map: int32 [8, 2048], P('req', 'tok'), may hold values from -1 to 4095, as said below
- w_out: bfloat16 [2048, 2048], replicated, may hold values from -0.125 to 0.125
- b_out: float32 [2048], replicated, may hold values from -4 to 4
- ln_gain: float32 [2048], replicated, may hold values from 0.1 to 1.9
- ln_bias: float32 [2048], replicated, may hold values from -4 to 4
- w_up: bfloat16 [2048, 8192], P(None, 'tok'), may hold values from -0.125 to 0.125
- b_up: float32 [8192], P('tok'), may hold values from -6 to 6
- w_down: bfloat16 [8192, 2048], P('tok'), may hold values from -0.0625 to 0.0625
- b_down: float32 [2048], replicated, may hold values from -4 to 4
Outputs:
- layer_out: bfloat16 [4096, 2048], P(('req', 'tok'))
Inputs may be any that keep to these rules, and one draw needn't show every extreme that they name: `prefix_len`: some request uses all 4096 cached positions. In each request the slots that are not -1 are its first n, with n from 128 to 2048; the n over all requests sum to 4096 and the largest is exactly 2048. These slots hold distinct rows of layer_out, every row held by exactly one of them. The live slots of one device's block of dest_map name at most 16 rows of any one device's block of layer_out.
All inputs are finite; a program needn't handle non-finite values.
Results may differ from a plain program's by a relative error of at most 0.012.
Values may be sent and summed in bfloat16 or wider, within the bound.
No kernel may reach another device: no remote copies, remote signals or barrier semaphores. Data moves between devices by JAX's collectives and lax.ppermute only.
A program may use at most 192 MiB of HBM per device.

v0:
```python
import math
import jax
import jax.numpy as jnp
from jax import lax
from jax.sharding import PartitionSpec as P

TOK_DEV = 128
neg_large = -1e30
ln_eps = 1e-05


def attend_block(
    state, block, block_start, queries_four, query_pos, own_prefix, shard_keys, shard_prefix, scale
):
    running_max, running_sum, accum = state
    count = block.shape[1]
    head_dim = queries_four.shape[-1]
    index_all = block_start + jnp.arange(count, dtype=jnp.int32)
    owner = index_all // shard_keys
    offset = index_all % shard_keys
    in_prefix = offset < shard_prefix
    prefix_pos = owner * shard_prefix + offset
    new_pos = owner * (shard_keys - shard_prefix) + offset - shard_prefix
    prefix_seen = prefix_pos[None, None, :] < own_prefix[:, None, None]
    new_seen = new_pos[None, None, :] <= query_pos[None, :, None]
    visible = jnp.where(in_prefix[None, None, :], prefix_seen, new_seen)[:, None, :, :]
    scores = (
        jnp.einsum(
            "rqhd,rkd->rhqk",
            queries_four,
            block[:, :, :head_dim],
            preferred_element_type=jnp.float32,
        )
        * scale
    )
    scores = jnp.where(visible, scores, neg_large)
    new_max = jnp.maximum(running_max, jnp.max(scores, axis=-1))
    probs = jnp.where(visible, jnp.exp(scores - new_max[..., None]), 0.0)
    factor = jnp.exp(running_max - new_max)
    new_sum = running_sum * factor + jnp.sum(probs, axis=-1)
    update = jnp.einsum(
        "rhqk,rkd->rhqd",
        probs.astype(jnp.bfloat16),
        block[:, :, head_dim:],
        preferred_element_type=jnp.float32,
    )
    return (new_max, new_sum, accum * factor[..., None] + update)


def project_rows(attended, residual_rows, w_out, b_out):
    total = (
        residual_rows.astype(jnp.float32)
        + jnp.dot(attended, w_out, preferred_element_type=jnp.float32)
        + b_out
    )
    return total.astype(jnp.bfloat16)


def per_device(
    queries,
    new_kv,
    cache_kv,
    residual,
    prefix_len,
    dest_map,
    w_out,
    b_out,
    ln_gain,
    ln_bias,
    w_up,
    b_up,
    w_down,
    b_down,
):
    group = lax.axis_index("req")
    member = lax.axis_index("tok")
    n_group = lax.axis_size("req")
    n_member = lax.axis_size("tok")
    devices = n_group * n_member
    req_dev, slot_dev, width = queries.shape
    head_dim = new_kv.shape[2] // 2
    heads = width // head_dim
    prefix_dev = cache_kv.shape[1]
    shard_keys = prefix_dev + slot_dev
    own_prefix = lax.dynamic_slice_in_dim(prefix_len, group * req_dev, req_dev)
    query_pos = member * slot_dev + jnp.arange(slot_dev, dtype=jnp.int32)
    queries_four = queries.reshape(req_dev, slot_dev, heads, head_dim)
    scale = 1.0 / math.sqrt(head_dim)
    local_keys = jnp.concatenate([cache_kv, new_kv], axis=1)

    def attend(state, block, block_start):
        return attend_block(
            state,
            block,
            block_start,
            queries_four,
            query_pos,
            own_prefix,
            shard_keys,
            prefix_dev,
            scale,
        )

    initial = (
        jnp.full((req_dev, heads, slot_dev), neg_large, jnp.float32),
        jnp.zeros((req_dev, heads, slot_dev), jnp.float32),
        jnp.zeros((req_dev, heads, slot_dev, head_dim), jnp.float32),
    )
    state = initial
    piece = lax.all_gather(local_keys, "tok", axis=1, tiled=True)
    count = piece.shape[1]
    number = count // shard_keys
    blocks = jnp.moveaxis(piece.reshape(req_dev, number, shard_keys, piece.shape[2]), 1, 0)

    def one_block(carry, item):
        block, index = item
        return (attend(carry, block, index * shard_keys), None)

    state, unused = lax.scan(one_block, state, (blocks, jnp.arange(number, dtype=jnp.int32)))
    running_max, running_sum, accum = state
    attended = (accum / running_sum[..., None]).astype(jnp.bfloat16)
    slots = req_dev * slot_dev
    attended = jnp.transpose(attended, (0, 2, 1, 3)).reshape(slots, width)
    residual_flat = residual.reshape(slots, width)
    capacity = (slots + devices - 1) // devices
    target = dest_map.reshape(slots)
    is_live = target >= 0
    peer = jnp.where(is_live, target // TOK_DEV, devices)
    onehot = (peer[:, None] == jnp.arange(devices, dtype=jnp.int32)[None, :]).astype(jnp.int32)
    position = jnp.sum((jnp.cumsum(onehot, axis=0) - 1) * onehot, axis=1)
    where_to = jnp.where(is_live, peer * capacity + position, devices * capacity)
    row_ids = (
        jnp.full((devices * capacity,), -1, jnp.int32)
        .at[where_to]
        .set(target % TOK_DEV, mode="drop")
    )
    payload = jnp.stack([attended, residual_flat], axis=1)
    layers = payload.shape[1]
    send_rows = (
        jnp.zeros((devices * capacity, layers, width), jnp.bfloat16)
        .at[where_to]
        .set(payload, mode="drop")
    )
    rows_in, ids_in = (
        lax.all_to_all(
            send_rows.reshape(devices, capacity, layers, width),
            ("req", "tok"),
            split_axis=0,
            concat_axis=0,
            tiled=True,
        ),
        lax.all_to_all(
            row_ids.reshape(devices, capacity),
            ("req", "tok"),
            split_axis=0,
            concat_axis=0,
            tiled=True,
        ),
    )
    rows_in = rows_in.reshape(devices * capacity, layers, width)
    ids_in = ids_in.reshape(devices * capacity)
    landing = jnp.where(ids_in >= 0, ids_in, TOK_DEV)
    even_rows = (
        jnp.zeros((TOK_DEV, layers, width), jnp.bfloat16).at[landing].set(rows_in, mode="drop")
    )
    hidden_state = project_rows(even_rows[:, 0], even_rows[:, 1], w_out, b_out)
    state_f = hidden_state.astype(jnp.float32)
    mean = jnp.mean(state_f, axis=-1, keepdims=True)
    centered = state_f - mean
    variance = jnp.mean(centered * centered, axis=-1, keepdims=True)
    normed = (centered * lax.rsqrt(variance + ln_eps) * ln_gain + ln_bias).astype(jnp.bfloat16)
    units = jax.nn.gelu(
        jnp.dot(
            lax.all_gather(normed, "tok", axis=0, tiled=True),
            w_up,
            preferred_element_type=jnp.float32,
        )
        + b_up,
        approximate=True,
    )
    terms = jnp.dot(units.astype(jnp.bfloat16), w_down, preferred_element_type=jnp.float32)
    summed = lax.psum_scatter(
        terms.astype(jnp.bfloat16), "tok", scatter_dimension=0, tiled=True
    ).astype(jnp.float32)
    return (state_f + summed + b_down).astype(jnp.bfloat16)


def solution(mesh):
    in_specs = (
        P("req", "tok", None),
        P("req", "tok", None),
        P("req", "tok", None),
        P("req", "tok", None),
        P(),
        P("req", "tok"),
        P(),
        P(),
        P(),
        P(),
        P(None, "tok"),
        P("tok"),
        P("tok", None),
        P(),
    )
    out_specs = P(("req", "tok"), None)
    return jax.shard_map(
        per_device, mesh=mesh, in_specs=in_specs, out_specs=out_specs, check_vma=False
    )
```

profile of v0, /device:TPU:0, one launch (start us, length us, event | category | flops | bytes accessed | tf_op | source)
XLA Modules:
  0.0 847.8 jit_solution(4371409342720919751)
XLA Ops:
  6.5 2.2 pad_maximum_fusion.1
  8.8 0.7 reshape.310
  9.5 1.2 reduce-window.6
  11.0 0.7 copy.49
  11.6 0.7 copy.48
  12.5 2.4 scatter_custom_fusion
  14.9 0.7 all_to_all.9
  15.6 7.4 all-to-all-start
  23.1 2.5 copy.35
  25.6 3.0 copy.37
  28.8 82.8 %all-gather.3.cloned.1.call-done = bf16[2,6144,256]{2,1,0:T(8,128)(2,1)} async-done(((bf16[2,768,256]{2,1,0:T(8,128)(2,1)}), bf16[2,6144,256]{2,1,0:T(8,128)(2,1)}) %all-gather.3.cloned.1.call-update) | async-done | bytes 6291472 | tf_op jit(solution)/shard_map/all_gather | solution.py:110
  111.6 320.0 %while.17 = (s32[]{:T(128)}, f32[2,16,256]{2,1,0:T(8,128)S(1)}, f32[2,16,256]{2,1,0:T(8,128)S(1)}, f32[2,16,256,128]{3,2,1,0:T(8,128)}, s32[8]{0:T(128)S(1)}, /*...) while((s32[]{:T(128)}, f32[2,16,256]{2,1,0:T(8,128)S(1)}, ...), condition=%wide.region_7.8_spmd.clone, body=%wide.region_4.7_spmd.clone.sunk | while | flops 3306812672 | bytes 90852008 | solution.py:119
  111.6 0.7 dynamic_slice.24
  113.9 1.2 dynamic-slice_bitcast_fusion.2
  115.1 10.2 %fusion.77 = (f32[2,16,256]{2,1,0:T(8,128)S(1)}, f32[2,768,256,16]{2,1,3,0:T(8,128)}) fusion(pred[2,256,768]{1,2,0:T(8,128)(4,1)S(1)} %broadcast_select_fusion.2, bf16[2,256,16,128]{3,1,2,0:T(8,128)(2,1)S(1)} %get-tuple-element.313, bf16[2,768,256]{2,1,0:T(8,128)(2,1)S(1)} %dynamic-slice_bitcast_fusion.2), kind=kOutput, calls=%fused_computation.6.clone.1 | convolution fusion | flops 1629478912 | bytes 28082176 | tf_op jit(solution)/shard_map/while/body/eval_jaxpr/rqhd,rkd->rhqk/dot_general | solution.py:28
  125.3 11.4 %fusion.78 = f32[2,16,256]{2,1,0:T(8,128)S(1)} fusion(f32[2,768,256,16]{2,1,3,0:T(8,128)} %get-tuple-element.279, f32[2,16,256]{2,1,0:T(8,128)S(1)} %select_maximum_fusion.2, pred[2,256,768]{1,2,0:T(8,128)(4,1)S(1)} %broadcast_select_fusion.2), kind=kLoop, calls=%fused_computation.8.clone.1 | loop fusion | flops 31449088 | bytes 25624576 | tf_op jit(solution)/shard_map/while/body/eval_jaxpr/reduce_sum | solution.py:40
  136.8 14.3 %fusion.80 = f32[2,16,256,128]{3,2,1,0:T(8,128)} fusion(f32[2,16,256,128]{3,2,1,0:T(8,128)} %get-tuple-element.297, f32[2,16,256]{2,1,0:T(8,128)S(1)} %get-tuple-element.281, pred[]{:T(512)S(6)} %compare.19, f32[2,768,256,16]{2,1,3,0:T(8,128)} %get-tuple-element.279, f32[2,16,256]{2,1,0:T(8,128)S(1)} %select_maximum_fusion.2, ...), kind=kOutput, calls=%fused_computation.12.clone.1 | convolution fusion | flops 1645215744 | bytes 34406400 | tf_op jit(solution)/shard_map/while/body/eval_jaxpr/rhqk,rkd->rhqd/dot_general | solution.py:41
  153.4 1.2 dynamic-slice_bitcast_fusion.2
  154.6 10.2 %fusion.77 = (f32[2,16,256]{2,1,0:T(8,128)S(1)}, f32[2,768,256,16]{2,1,3,0:T(8,128)}) fusion(pred[2,256,768]{1,2,0:T(8,128)(4,1)S(1)} %broadcast_select_fusion.2, bf16[2,256,16,128]{3,1,2,0:T(8,128)(2,1)S(1)} %get-tuple-element.313, bf16[2,768,256]{2,1,0:T(8,128)(2,1)S(1)} %dynamic-slice_bitcast_fusion.2), kind=kOutput, calls=%fused_computation.6.clone.1 | convolution fusion | flops 1629478912 | bytes 28082176 | tf_op jit(solution)/shard_map/while/body/eval_jaxpr/rqhd,rkd->rhqk/dot_general | solution.py:28
  164.8 11.4 %fusion.78 = f32[2,16,256]{2,1,0:T(8,128)S(1)} fusion(f32[2,768,256,16]{2,1,3,0:T(8,128)} %get-tuple-element.279, f32[2,16,256]{2,1,0:T(8,128)S(1)} %select_maximum_fusion.2, pred[2,256,768]{1,2,0:T(8,128)(4,1)S(1)} %broadcast_select_fusion.2), kind=kLoop, calls=%fused_computation.8.clone.1 | loop fusion | flops 31449088 | bytes 25624576 | tf_op jit(solution)/shard_map/while/body/eval_jaxpr/reduce_sum | solution.py:40
  176.3 14.9 %fusion.80 = f32[2,16,256,128]{3,2,1,0:T(8,128)} fusion(f32[2,16,256,128]{3,2,1,0:T(8,128)} %get-tuple-element.297, f32[2,16,256]{2,1,0:T(8,128)S(1)} %get-tuple-element.281, pred[]{:T(512)S(6)} %compare.19, f32[2,768,256,16]{2,1,3,0:T(8,128)} %get-tuple-element.279, f32[2,16,256]{2,1,0:T(8,128)S(1)} %select_maximum_fusion.2, ...), kind=kOutput, calls=%fused_computation.12.clone.1 | convolution fusion | flops 1645215744 | bytes 34406400 | tf_op jit(solution)/shard_map/while/body/eval_jaxpr/rhqk,rkd->rhqd/dot_general | solution.py:41
  193.4 1.2 dynamic-slice_bitcast_fusion.2
  194.6 10.2 %fusion.77 = (f32[2,16,256]{2,1,0:T(8,128)S(1)}, f32[2,768,256,16]{2,1,3,0:T(8,128)}) fusion(pred[2,256,768]{1,2,0:T(8,128)(4,1)S(1)} %broadcast_select_fusion.2, bf16[2,256,16,128]{3,1,2,0:T(8,128)(2,1)S(1)} %get-tuple-element.313, bf16[2,768,256]{2,1,0:T(8,128)(2,1)S(1)} %dynamic-slice_bitcast_fusion.2), kind=kOutput, calls=%fused_computation.6.clone.1 | convolution fusion | flops 1629478912 | bytes 28082176 | tf_op jit(solution)/shard_map/while/body/eval_jaxpr/rqhd,rkd->rhqk/dot_general | solution.py:28
  204.9 11.4 %fusion.78 = f32[2,16,256]{2,1,0:T(8,128)S(1)} fusion(f32[2,768,256,16]{2,1,3,0:T(8,128)} %get-tuple-element.279, f32[2,16,256]{2,1,0:T(8,128)S(1)} %select_maximum_fusion.2, pred[2,256,768]{1,2,0:T(8,128)(4,1)S(1)} %broadcast_select_fusion.2), kind=kLoop, calls=%fused_computation.8.clone.1 | loop fusion | flops 31449088 | bytes 25624576 | tf_op jit(solution)/shard_map/while/body/eval_jaxpr/reduce_sum | solution.py:40
  216.3 14.9 %fusion.80 = f32[2,16,256,128]{3,2,1,0:T(8,128)} fusion(f32[2,16,256,128]{3,2,1,0:T(8,128)} %get-tuple-element.297, f32[2,16,256]{2,1,0:T(8,128)S(1)} %get-tuple-element.281, pred[]{:T(512)S(6)} %compare.19, f32[2,768,256,16]{2,1,3,0:T(8,128)} %get-tuple-element.279, f32[2,16,256]{2,1,0:T(8,128)S(1)} %select_maximum_fusion.2, ...), kind=kOutput, calls=%fused_computation.12.clone.1 | convolution fusion | flops 1645215744 | bytes 34406400 | tf_op jit(solution)/shard_map/while/body/eval_jaxpr/rhqk,rkd->rhqd/dot_general | solution.py:41
  233.5 1.2 dynamic-slice_bitcast_fusion.2
  234.7 10.2 %fusion.77 = (f32[2,16,256]{2,1,0:T(8,128)S(1)}, f32[2,768,256,16]{2,1,3,0:T(8,128)}) fusion(pred[2,256,768]{1,2,0:T(8,128)(4,1)S(1)} %broadcast_select_fusion.2, bf16[2,256,16,128]{3,1,2,0:T(8,128)(2,1)S(1)} %get-tuple-element.313, bf16[2,768,256]{2,1,0:T(8,128)(2,1)S(1)} %dynamic-slice_bitcast_fusion.2), kind=kOutput, calls=%fused_computation.6.clone.1 | convolution fusion | flops 1629478912 | bytes 28082176 | tf_op jit(solution)/shard_map/while/body/eval_jaxpr/rqhd,rkd->rhqk/dot_general | solution.py:28
  245.0 11.4 %fusion.78 = f32[2,16,256]{2,1,0:T(8,128)S(1)} fusion(f32[2,768,256,16]{2,1,3,0:T(8,128)} %get-tuple-element.279, f32[2,16,256]{2,1,0:T(8,128)S(1)} %select_maximum_fusion.2, pred[2,256,768]{1,2,0:T(8,128)(4,1)S(1)} %broadcast_select_fusion.2), kind=kLoop, calls=%fused_computation.8.clone.1 | loop fusion | flops 31449088 | bytes 25624576 | tf_op jit(solution)/shard_map/while/body/eval_jaxpr/reduce_sum | solution.py:40
  256.4 14.9 %fusion.80 = f32[2,16,256,128]{3,2,1,0:T(8,128)} fusion(f32[2,16,256,128]{3,2,1,0:T(8,128)} %get-tuple-element.297, f32[2,16,256]{2,1,0:T(8,128)S(1)} %get-tuple-element.281, pred[]{:T(512)S(6)} %compare.19, f32[2,768,256,16]{2,1,3,0:T(8,128)} %get-tuple-element.279, f32[2,16,256]{2,1,0:T(8,128)S(1)} %select_maximum_fusion.2, ...), kind=kOutput, calls=%fused_computation.12.clone.1 | convolution fusion | flops 1645215744 | bytes 34406400 | tf_op jit(solution)/shard_map/while/body/eval_jaxpr/rhqk,rkd->rhqd/dot_general | solution.py:41
  273.6 1.2 dynamic-slice_bitcast_fusion.2
  274.8 10.2 %fusion.77 = (f32[2,16,256]{2,1,0:T(8,128)S(1)}, f32[2,768,256,16]{2,1,3,0:T(8,128)}) fusion(pred[2,256,768]{1,2,0:T(8,128)(4,1)S(1)} %broadcast_select_fusion.2, bf16[2,256,16,128]{3,1,2,0:T(8,128)(2,1)S(1)} %get-tuple-element.313, bf16[2,768,256]{2,1,0:T(8,128)(2,1)S(1)} %dynamic-slice_bitcast_fusion.2), kind=kOutput, calls=%fused_computation.6.clone.1 | convolution fusion | flops 1629478912 | bytes 28082176 | tf_op jit(solution)/shard_map/while/body/eval_jaxpr/rqhd,rkd->rhqk/dot_general | solution.py:28
  285.1 11.4 %fusion.78 = f32[2,16,256]{2,1,0:T(8,128)S(1)} fusion(f32[2,768,256,16]{2,1,3,0:T(8,128)} %get-tuple-element.279, f32[2,16,256]{2,1,0:T(8,128)S(1)} %select_maximum_fusion.2, pred[2,256,768]{1,2,0:T(8,128)(4,1)S(1)} %broadcast_select_fusion.2), kind=kLoop, calls=%fused_computation.8.clone.1 | loop fusion | flops 31449088 | bytes 25624576 | tf_op jit(solution)/shard_map/while/body/eval_jaxpr/reduce_sum | solution.py:40
  296.5 14.9 %fusion.80 = f32[2,16,256,128]{3,2,1,0:T(8,128)} fusion(f32[2,16,256,128]{3,2,1,0:T(8,128)} %get-tuple-element.297, f32[2,16,256]{2,1,0:T(8,128)S(1)} %get-tuple-element.281, pred[]{:T(512)S(6)} %compare.19, f32[2,768,256,16]{2,1,3,0:T(8,128)} %get-tuple-element.279, f32[2,16,256]{2,1,0:T(8,128)S(1)} %select_maximum_fusion.2, ...), kind=kOutput, calls=%fused_computation.12.clone.1 | convolution fusion | flops 1645215744 | bytes 34406400 | tf_op jit(solution)/shard_map/while/body/eval_jaxpr/rhqk,rkd->rhqd/dot_general | solution.py:41
  311.4 0.7 dynamic_slice.24
  313.7 1.2 dynamic-slice_bitcast_fusion.2
  314.9 10.2 %fusion.77 = (f32[2,16,256]{2,1,0:T(8,128)S(1)}, f32[2,768,256,16]{2,1,3,0:T(8,128)}) fusion(pred[2,256,768]{1,2,0:T(8,128)(4,1)S(1)} %broadcast_select_fusion.2, bf16[2,256,16,128]{3,1,2,0:T(8,128)(2,1)S(1)} %get-tuple-element.313, bf16[2,768,256]{2,1,0:T(8,128)(2,1)S(1)} %dynamic-slice_bitcast_fusion.2), kind=kOutput, calls=%fused_computation.6.clone.1 | convolution fusion | flops 1629478912 | bytes 28082176 | tf_op jit(solution)/shard_map/while/body/eval_jaxpr/rqhd,rkd->rhqk/dot_general | solution.py:28
  325.1 11.4 %fusion.78 = f32[2,16,256]{2,1,0:T(8,128)S(1)} fusion(f32[2,768,256,16]{2,1,3,0:T(8,128)} %get-tuple-element.279, f32[2,16,256]{2,1,0:T(8,128)S(1)} %select_maximum_fusion.2, pred[2,256,768]{1,2,0:T(8,128)(4,1)S(1)} %broadcast_select_fusion.2), kind=kLoop, calls=%fused_computation.8.clone.1 | loop fusion | flops 31449088 | bytes 25624576 | tf_op jit(solution)/shard_map/while/body/eval_jaxpr/reduce_sum | solution.py:40
  336.6 14.9 %fusion.80 = f32[2,16,256,128]{3,2,1,0:T(8,128)} fusion(f32[2,16,256,128]{3,2,1,0:T(8,128)} %get-tuple-element.297, f32[2,16,256]{2,1,0:T(8,128)S(1)} %get-tuple-element.281, pred[]{:T(512)S(6)} %compare.19, f32[2,768,256,16]{2,1,3,0:T(8,128)} %get-tuple-element.279, f32[2,16,256]{2,1,0:T(8,128)S(1)} %select_maximum_fusion.2, ...), kind=kOutput, calls=%fused_computation.12.clone.1 | convolution fusion | flops 1645215744 | bytes 34406400 | tf_op jit(solution)/shard_map/while/body/eval_jaxpr/rhqk,rkd->rhqd/dot_general | solution.py:41
  353.8 1.2 dynamic-slice_bitcast_fusion.2
  355.0 10.2 %fusion.77 = (f32[2,16,256]{2,1,0:T(8,128)S(1)}, f32[2,768,256,16]{2,1,3,0:T(8,128)}) fusion(pred[2,256,768]{1,2,0:T(8,128)(4,1)S(1)} %broadcast_select_fusion.2, bf16[2,256,16,128]{3,1,2,0:T(8,128)(2,1)S(1)} %get-tuple-element.313, bf16[2,768,256]{2,1,0:T(8,128)(2,1)S(1)} %dynamic-slice_bitcast_fusion.2), kind=kOutput, calls=%fused_computation.6.clone.1 | convolution fusion | flops 1629478912 | bytes 28082176 | tf_op jit(solution)/shard_map/while/body/eval_jaxpr/rqhd,rkd->rhqk/dot_general | solution.py:28
  365.2 11.4 %fusion.78 = f32[2,16,256]{2,1,0:T(8,128)S(1)} fusion(f32[2,768,256,16]{2,1,3,0:T(8,128)} %get-tuple-element.279, f32[2,16,256]{2,1,0:T(8,128)S(1)} %select_maximum_fusion.2, pred[2,256,768]{1,2,0:T(8,128)(4,1)S(1)} %broadcast_select_fusion.2), kind=kLoop, calls=%fused_computation.8.clone.1 | loop fusion | flops 31449088 | bytes 25624576 | tf_op jit(solution)/shard_map/while/body/eval_jaxpr/reduce_sum | solution.py:40
  376.7 14.9 %fusion.80 = f32[2,16,256,128]{3,2,1,0:T(8,128)} fusion(f32[2,16,256,128]{3,2,1,0:T(8,128)} %get-tuple-element.297, f32[2,16,256]{2,1,0:T(8,128)S(1)} %get-tuple-element.281, pred[]{:T(512)S(6)} %compare.19, f32[2,768,256,16]{2,1,3,0:T(8,128)} %get-tuple-element.279, f32[2,16,256]{2,1,0:T(8,128)S(1)} %select_maximum_fusion.2, ...), kind=kOutput, calls=%fused_computation.12.clone.1 | convolution fusion | flops 1645215744 | bytes 34406400 | tf_op jit(solution)/shard_map/while/body/eval_jaxpr/rhqk,rkd->rhqd/dot_general | solution.py:41
  393.8 1.2 dynamic-slice_bitcast_fusion.2
  395.0 10.2 %fusion.77 = (f32[2,16,256]{2,1,0:T(8,128)S(1)}, f32[2,768,256,16]{2,1,3,0:T(8,128)}) fusion(pred[2,256,768]{1,2,0:T(8,128)(4,1)S(1)} %broadcast_select_fusion.2, bf16[2,256,16,128]{3,1,2,0:T(8,128)(2,1)S(1)} %get-tuple-element.313, bf16[2,768,256]{2,1,0:T(8,128)(2,1)S(1)} %dynamic-slice_bitcast_fusion.2), kind=kOutput, calls=%fused_computation.6.clone.1 | convolution fusion | flops 1629478912 | bytes 28082176 | tf_op jit(solution)/shard_map/while/body/eval_jaxpr/rqhd,rkd->rhqk/dot_general | solution.py:28
  405.3 11.4 %fusion.78 = f32[2,16,256]{2,1,0:T(8,128)S(1)} fusion(f32[2,768,256,16]{2,1,3,0:T(8,128)} %get-tuple-element.279, f32[2,16,256]{2,1,0:T(8,128)S(1)} %select_maximum_fusion.2, pred[2,256,768]{1,2,0:T(8,128)(4,1)S(1)} %broadcast_select_fusion.2), kind=kLoop, calls=%fused_computation.8.clone.1 | loop fusion | flops 31449088 | bytes 25624576 | tf_op jit(solution)/shard_map/while/body/eval_jaxpr/reduce_sum | solution.py:40
  416.7 14.9 %fusion.80 = f32[2,16,256,128]{3,2,1,0:T(8,128)} fusion(f32[2,16,256,128]{3,2,1,0:T(8,128)} %get-tuple-element.297, f32[2,16,256]{2,1,0:T(8,128)S(1)} %get-tuple-element.281, pred[]{:T(512)S(6)} %compare.19, f32[2,768,256,16]{2,1,3,0:T(8,128)} %get-tuple-element.279, f32[2,16,256]{2,1,0:T(8,128)S(1)} %select_maximum_fusion.2, ...), kind=kOutput, calls=%fused_computation.12.clone.1 | convolution fusion | flops 1645215744 | bytes 34406400 | tf_op jit(solution)/shard_map/while/body/eval_jaxpr/rhqk,rkd->rhqd/dot_general | solution.py:41
  431.6 2.9 fusion.39
  434.5 1.4 copy.38
  435.9 2.3 stack_reshape.6
  438.2 2.6 pad_maximum_fusion
  440.8 6.3 copy.39
  447.1 4.1 broadcast_in_dim.112
  451.2 64.2 %scatter_fusion = bf16[512,2,2048]{2,1,0:T(2,128)(2,1)} fusion(bf16[512,2,2048]{2,1,0:T(2,128)(2,1)} %broadcast_in_dim.112, s32[512]{0:T(512)S(1)} %bitcast.107, bf16[512,2,2048]{2,1,0:T(2,128)(2,1)} %copy.39), kind=kCustom, calls=%fused_computation.1 | custom fusion | bytes 12584960 | tf_op jit(solution)/shard_map/scatter | solution.py:142
  515.4 3.6 all-to-all-start.1
  519.5 1.4 reduce.5
  521.0 93.9 %all-to-all-done.1 = bf16[32,16,2,2048]{3,2,1,0:T(2,128)(2,1)} async-done(((bf16[32,16,2,2048]{3,2,1,0:T(2,128)(2,1)}), bf16[32,16,2,2048]{3,2,1,0:T(2,128)(2,1)}, u32[]{:S(2)}, u32[]{:S(2)}) %all-to-all-start.1) | async-done | bytes 4194336 | tf_op jit(solution)/shard_map/all_to_all | solution.py:145
  615.5 43.0 %scatter_fusion.1 = bf16[128,2,2048]{2,1,0:T(2,128)(2,1)S(1)} fusion(bf16[128,2,2048]{2,1,0:T(2,128)(2,1)S(1)} %broadcast_in_dim.106, s32[512]{0:T(512)S(1)} %bitcast.108, bf16[512,2,2048]{2,1,0:T(2,128)(2,1)} %bitcast.11), kind=kCustom, calls=%fused_computation.2 | custom fusion | bytes 12584960 | tf_op jit(solution)/shard_map/scatter | solution.py:164
  658.5 1.5 fusion.60
  660.1 5.5 fusion.61
  665.8 1.0 add_convert_fusion.1
  667.0 70.8 %all-gather.5.cloned.1.call-done = bf16[1024,2048]{1,0:T(8,128)(2,1)} async-done(((bf16[128,2048]{1,0:T(8,128)(2,1)}), bf16[1024,2048]{1,0:T(8,128)(2,1)}) %all-gather.5.cloned.1.call-update) | async-done | bytes 4194320 | tf_op jit(solution)/shard_map/all_gather | solution.py:174
  737.7 15.3 %convolution_convert_fusion = bf16[1024,2048]{1,0:T(8,128)(2,1)} fusion(bf16[1024,2048]{1,0:T(8,128)(2,1)} %param.28, f32[1024]{0:T(1024)S(1)} %copy-done.7, bf16[1024,2048]{1,0:T(8,128)(2,1)} %all-gather.5.cloned.1.call-done, bf16[2048,1024]{1,0:T(8,128)(2,1)} %param.26), kind=kOutput, calls=%fused_computation.51 | convolution fusion | flops 8602517504 | bytes 16781312 | tf_op jit(solution)/shard_map/dot_general | solution.py:181
  753.0 86.3 %reduce-scatter.2.cloned.1.call-done = bf16[128,2048]{1,0:T(8,128)(2,1)} async-done(((bf16[1024,2048]{1,0:T(8,128)(2,1)}), bf16[128,2048]{1,0:T(8,128)(2,1)}) %reduce-scatter.2.cloned.1.call-update) | async-done | bytes 524304 | tf_op jit(solution)/shard_map/reduce_scatter | solution.py:182
  839.3 2.0 add_convert_fusion
  (123 shorter events, 13.4 us)
Async XLA Ops:
  6.5 16.5 %copy-start = (bf16[2,256,2048]{2,1,0:T(8,128)(2,1)S(1)}, bf16[2,256,2048]{2,1,0:T(8,128)(2,1)}, u32[]{:S(2)}) copy-start(bf16[2,256,2048]{2,1,0:T(8,128)(2,1)} %param.16) | copy-start | bytes 6291460
  6.5 105.1 %all-gather.3.cloned.1.call-start = ((), (), s32[]{:S(2)}) async-start(), calls=%async_computation.3 | async-start | bytes 7077888 | tf_op jit(solution)/shard_map/all_gather | solution.py:110
  12.5 16.2 %copy-start.5 = (s32[512,1]{0,1:T(1,128)}, s32[512,1]{0,1:T(1,128)S(1)}, u32[]{:S(2)}) copy-start(s32[512,1]{0,1:T(1,128)S(1)} %compare_select_fusion.2) | copy-start | bytes 6148
  15.6 499.8 %all-to-all-start = ((s32[32,1,16]{2,1,0:T(1,128)}), s32[32,1,16]{2,1,0:T(1,128)}, u32[]{:S(2)}, u32[]{:S(2)}) async-start(s32[32,1,16]{2,1,0:T(1,128)} %bitcast.3), calls=%async_computation | async-start | bytes 32768 | tf_op jit(solution)/shard_map/all_to_all | solution.py:152
  23.1 5.6 copy-start.8
  447.1 4.1 copy-start.6
  515.4 99.5 %all-to-all-start.1 = ((bf16[32,16,2,2048]{3,2,1,0:T(2,128)(2,1)}), bf16[32,16,2,2048]{3,2,1,0:T(2,128)(2,1)}, u32[]{:S(2)}, u32[]{:S(2)}) async-start(bf16[32,16,2,2048]{3,2,1,0:T(2,128)(2,1)} %bitcast.97), calls=%async_computation.1 | async-start | bytes 8388608 | tf_op jit(solution)/shard_map/all_to_all | solution.py:145
  519.0 218.8 %all-gather.5.cloned.1.call-start = ((), (), s32[]{:S(2)}) async-start(), calls=%async_computation.4 | async-start | bytes 4718592 | tf_op jit(solution)/shard_map/all_gather | solution.py:174
  658.5 1.5 copy-start.1
  660.1 5.8 copy-start.2
  660.1 5.8 copy-start.3
  660.1 77.7 %copy-start.7 = (f32[1024]{0:T(1024)S(1)}, f32[1024]{0:T(1024)}, u32[]{:S(2)}) copy-start(f32[1024]{0:T(1024)} %param.27) | copy-start | bytes 12292
  666.9 172.4 %reduce-scatter.2.cloned.1.call-start = ((), (), s32[]{:S(2)}) async-start(), calls=%async_computation.5 | async-start | bytes 4718592 | tf_op jit(solution)/shard_map/reduce_scatter | solution.py:182
  753.0 86.3 %copy-start.4 = (f32[2048]{0:T(1024)S(1)}, f32[2048]{0:T(1024)}, u32[]{:S(2)}) copy-start(f32[2048]{0:T(1024)} %param.29) | copy-start | bytes 24580
Sparse Core Ops, SparseCore 0:
  9.6 101.9 all-gather.2
  667.0 70.6 all-gather.4
  753.1 86.1 reduce-scatter.1
where the time goes:
time: 851 us; the launch traced here: 848 us
  waiting for transfers between devices  334 us (39%)
  matrix products  221 us (26%)
  local copies, waits for them, and re-layouts  150 us (18%)
  other arithmetic  112 us (13%)
  between operations  13.3 us (2%)
  starting transfers between devices  11.1 us (1%)
    dot_general x8, matrix products, attend_block(): jnp.einsum('rhqk,rkd->rhqd', probs.astype(jnp.bfloat16), block[:, :, head...  119 us
    all_to_all x1, waiting for transfers between devices, per_device(): lax.all_to_all(send_rows.reshape(devices, capacity, layers, width), ('req...  93.9 us
    reduce_sum x8, other arithmetic, attend_block(): new_sum = running_sum * factor + jnp.sum(probs, axis=-1)  91.3 us
    reduce_scatter x1, waiting for transfers between devices, per_device(): lax.psum_scatter(terms.astype(jnp.bfloat16), 'tok', scatter_dimension=0,...  86.3 us
    all_gather x1, waiting for transfers between devices, per_device(): piece = lax.all_gather(local_keys, 'tok', axis=1, tiled=True)  82.8 us
    dot_general x8, matrix products, attend_block(): jnp.einsum('rqhd,rkd->rhqk', queries_four, block[:, :, :head_dim], prefer...  82 us
    all_gather x1, waiting for transfers between devices, per_device(): lax.all_gather(normed, 'tok', axis=0, tiled=True)  70.8 us
    scatter x1, local copies, waits for them, and re-layouts, per_device(): send_rows = jnp.zeros((devices * capacity, layers, width), jnp.bfloat16)....  64.2 us
  transfers between devices with their start and end apart: 5, of which 4 were waited for; matrix products, arithmetic and copies ran while one was open for 49% of the time, Pallas kernels for 0%

commit v1 on v0

--- a/solution.py
+++ b/solution.py
@@ -107,7 +107,16 @@
         jnp.zeros((req_dev, heads, slot_dev, head_dim), jnp.float32),
     )
     state = initial
-    piece = lax.all_gather(local_keys, "tok", axis=1, tiled=True)
+    ways = lax.axis_size("tok")
+    up = [(d, (d + 1) % ways) for d in range(ways)]
+    down = [(d, (d - 1) % ways) for d in range(ways)]
+    earlier, later = ([local_keys], [local_keys])
+    for _ in range(ways // 2):
+        earlier.append(lax.ppermute(earlier[-1], "tok", up))
+    for _ in range((ways - 1) // 2):
+        later.append(lax.ppermute(later[-1], "tok", down))
+    line = jnp.concatenate([*earlier[::-1], *later[1:]], axis=1)
+    piece = jnp.roll(line, (lax.axis_index("tok") - ways // 2) * local_keys.shape[1], axis=1)
     count = piece.shape[1]
     number = count // shard_keys
     blocks = jnp.moveaxis(piece.reshape(req_dev, number, shard_keys, piece.shape[2]), 1, 0)

time: 851 us -> 892 us (1.048)
  starting transfers between devices: 11.1 us -> 41.2 us
  local copies, waits for them, and re-layouts: 150 us -> 172 us
  waiting for transfers between devices: 334 us -> 325 us
    all_gather x1 -> x0, waiting for transfers between devices: 82.8 us -> none  [per_device(): piece = lax.all_gather(local_keys, 'tok', axis=1, tiled=True)]
    ppermute x0 -> x7, waiting for transfers between devices: none -> 74.3 us  [the longest x4 64.1 us: per_device(): earlier.append(lax.ppermute(earlier[-1], 'tok', up))]
    ppermute x0 -> x7, starting transfers between devices: none -> 34.4 us  [the longest x3 26.3 us: per_device(): later.append(lax.ppermute(later[-1], 'tok', down))]
    unnamed x22 -> x48, local copies, waits for them, and re-layouts: 6.97 us -> 23.7 us
  transfers between devices with their start and end apart: 5 -> 11, of which waited for: 4 -> 7; matrix products, arithmetic and copies ran while one was open for 49% -> 48% of each run, Pallas kernels for 0% -> 0%
where the time goes in v1:
time: 892 us; the launch traced here: 889 us
  waiting for transfers between devices  325 us (36%)
  matrix products  221 us (25%)
  local copies, waits for them, and re-layouts  172 us (19%)
  other arithmetic  110 us (12%)
  starting transfers between devices  41.2 us (5%)
  between operations  13.8 us (2%)
    dot_general x8, matrix products, attend_block(): jnp.einsum('rhqk,rkd->rhqd', probs.astype(jnp.bfloat16), block[:, :, head...  119 us
    all_to_all x1, waiting for transfers between devices, per_device(): lax.all_to_all(send_rows.reshape(devices, capacity, layers, width), ('req...  93.9 us
    reduce_sum x8, other arithmetic, attend_block(): new_sum = running_sum * factor + jnp.sum(probs, axis=-1)  91.3 us
    reduce_scatter x1, waiting for transfers between devices, per_device(): lax.psum_scatter(terms.astype(jnp.bfloat16), 'tok', scatter_dimension=0,...  86.3 us
    dot_general x8, matrix products, attend_block(): jnp.einsum('rqhd,rkd->rhqk', queries_four, block[:, :, :head_dim], prefer...  81.9 us
    all_gather x1, waiting for transfers between devices, per_device(): lax.all_gather(normed, 'tok', axis=0, tiled=True)  70.8 us
    scatter x1, local copies, waits for them, and re-layouts, per_device(): send_rows = jnp.zeros((devices * capacity, layers, width), jnp.bfloat16)....  64.2 us
    ppermute x4, waiting for transfers between devices, per_device(): earlier.append(lax.ppermute(earlier[-1], 'tok', up))  64.1 us
  transfers between devices with their start and end apart: 11, of which 7 were waited for; matrix products, arithmetic and copies ran while one was open for 48% of the time, Pallas kernels for 0%

profile of v1, /device:TPU:0, one launch (start us, length us, event | category | flops | bytes accessed | tf_op | source)
XLA Modules:
  0.0 888.7 jit_solution(14206645193799168946)
XLA Ops:
  8.7 3.0 collective-permute-start
  11.8 20.6 %collective-permute-done = bf16[2,768,256]{2,1,0:T(8,128)(2,1)S(1)} collective-permute-done((bf16[2,768,256]{2,1,0:T(8,128)(2,1)S(1)}, bf16[2,768,256]{2,1,0:T(8,128)(2,1)S(1)}, u32[]{:S(2)}, u32[]{:S(2)}) %collective-permute-start) | collective-permute-done | bytes 786464 | tf_op jit(solution)/shard_map/ppermute | solution.py:115
  33.2 4.7 collective-permute-start.4
  38.0 28.7 %collective-permute-done.1 = bf16[2,768,256]{2,1,0:T(8,128)(2,1)S(1)} collective-permute-done((bf16[2,768,256]{2,1,0:T(8,128)(2,1)S(1)}, bf16[2,768,256]{2,1,0:T(8,128)(2,1)S(1)}, u32[]{:S(2)}, u32[]{:S(2)}) %collective-permute-start.1) | collective-permute-done | bytes 786464 | tf_op jit(solution)/shard_map/ppermute | solution.py:115
  66.6 2.5 collective-permute-start.2
  69.8 17.1 %collective-permute-start.5 = (bf16[2,768,256]{2,1,0:T(8,128)(2,1)}, bf16[2,768,256]{2,1,0:T(8,128)(2,1)}, u32[]{:S(2)}, u32[]{:S(2)}) collective-permute-start(bf16[2,768,256]{2,1,0:T(8,128)(2,1)} %collective-permute-done.4), channel_id=1, source_target_pairs={{0,7},{1,0},{2,1},{3,2},{4,3},{5,4},{6,5},{7,6},{8,15},{9,8},{10,9... | collective-permute-start | bytes 2359304 | tf_op jit(solution)/shard_map/ppermute | solution.py:117
  86.9 14.8 %collective-permute-done.2 = bf16[2,768,256]{2,1,0:T(8,128)(2,1)} collective-permute-done((bf16[2,768,256]{2,1,0:T(8,128)(2,1)S(1)}, bf16[2,768,256]{2,1,0:T(8,128)(2,1)}, u32[]{:S(2)}, u32[]{:S(2)}) %collective-permute-start.2) | collective-permute-done | bytes 786464 | tf_op jit(solution)/shard_map/ppermute | solution.py:115
  101.8 2.6 collective-permute-start.3
  107.3 2.4 scatter_custom_fusion
  110.4 3.2 all-to-all-start
  113.7 3.9 copy.35
  117.7 3.0 copy.37
  120.8 4.5 collective-permute-start.6
  132.5 10.2 %collective-permute-done.6 = bf16[2,768,256]{2,1,0:T(8,128)(2,1)S(1)} collective-permute-done((bf16[2,768,256]{2,1,0:T(8,128)(2,1)}, bf16[2,768,256]{2,1,0:T(8,128)(2,1)S(1)}, u32[]{:S(2)}, u32[]{:S(2)}) %collective-permute-start.6) | collective-permute-done | bytes 786464 | tf_op jit(solution)/shard_map/ppermute | solution.py:117
  148.9 4.2 constant_dynamic-slice_fusion
  153.1 319.0 %while.17 = (s32[]{:T(128)}, f32[2,16,256]{2,1,0:T(8,128)S(1)}, f32[2,16,256]{2,1,0:T(8,128)S(1)}, f32[2,16,256,128]{3,2,1,0:T(8,128)}, s32[8]{0:T(128)S(1)}, /*...) while((s32[]{:T(128)}, f32[2,16,256]{2,1,0:T(8,128)S(1)}, ...), condition=%wide.region_7.8_spmd.clone, body=%wide.region_4.7_spmd.clone.sunk | while | flops 3306812672 | bytes 90852008 | solution.py:128
  155.3 1.2 dynamic-slice_bitcast_fusion.2
  156.5 10.2 %fusion.77 = (f32[2,16,256]{2,1,0:T(8,128)S(1)}, f32[2,768,256,16]{2,1,3,0:T(8,128)}) fusion(pred[2,256,768]{1,2,0:T(8,128)(4,1)S(1)} %broadcast_select_fusion.2, bf16[2,256,16,128]{3,1,2,0:T(8,128)(2,1)S(1)} %get-tuple-element.313, bf16[2,768,256]{2,1,0:T(8,128)(2,1)S(1)} %dynamic-slice_bitcast_fusion.2), kind=kOutput, calls=%fused_computation.6.clone.1 | convolution fusion | flops 1629478912 | bytes 28082176 | tf_op jit(solution)/shard_map/while/body/eval_jaxpr/rqhd,rkd->rhqk/dot_general | solution.py:28
  166.7 11.4 %fusion.78 = f32[2,16,256]{2,1,0:T(8,128)S(1)} fusion(f32[2,768,256,16]{2,1,3,0:T(8,128)} %get-tuple-element.279, f32[2,16,256]{2,1,0:T(8,128)S(1)} %select_maximum_fusion.2, pred[2,256,768]{1,2,0:T(8,128)(4,1)S(1)} %broadcast_select_fusion.2), kind=kLoop, calls=%fused_computation.8.clone.1 | loop fusion | flops 31449088 | bytes 25624576 | tf_op jit(solution)/shard_map/while/body/eval_jaxpr/reduce_sum | solution.py:40
  178.2 14.3 %fusion.80 = f32[2,16,256,128]{3,2,1,0:T(8,128)} fusion(f32[2,16,256,128]{3,2,1,0:T(8,128)} %get-tuple-element.297, f32[2,16,256]{2,1,0:T(8,128)S(1)} %get-tuple-element.281, pred[]{:T(512)S(6)} %compare.19, f32[2,768,256,16]{2,1,3,0:T(8,128)} %get-tuple-element.279, f32[2,16,256]{2,1,0:T(8,128)S(1)} %select_maximum_fusion.2, ...), kind=kOutput, calls=%fused_computation.12.clone.1 | convolution fusion | flops 1645215744 | bytes 34406400 | tf_op jit(solution)/shard_map/while/body/eval_jaxpr/rhqk,rkd->rhqd/dot_general | solution.py:41
  194.7 1.2 dynamic-slice_bitcast_fusion.2
  195.9 10.2 %fusion.77 = (f32[2,16,256]{2,1,0:T(8,128)S(1)}, f32[2,768,256,16]{2,1,3,0:T(8,128)}) fusion(pred[2,256,768]{1,2,0:T(8,128)(4,1)S(1)} %broadcast_select_fusion.2, bf16[2,256,16,128]{3,1,2,0:T(8,128)(2,1)S(1)} %get-tuple-element.313, bf16[2,768,256]{2,1,0:T(8,128)(2,1)S(1)} %dynamic-slice_bitcast_fusion.2), kind=kOutput, calls=%fused_computation.6.clone.1 | convolution fusion | flops 1629478912 | bytes 28082176 | tf_op jit(solution)/shard_map/while/body/eval_jaxpr/rqhd,rkd->rhqk/dot_general | solution.py:28
  206.1 11.4 %fusion.78 = f32[2,16,256]{2,1,0:T(8,128)S(1)} fusion(f32[2,768,256,16]{2,1,3,0:T(8,128)} %get-tuple-element.279, f32[2,16,256]{2,1,0:T(8,128)S(1)} %select_maximum_fusion.2, pred[2,256,768]{1,2,0:T(8,128)(4,1)S(1)} %broadcast_select_fusion.2), kind=kLoop, calls=%fused_computation.8.clone.1 | loop fusion | flops 31449088 | bytes 25624576 | tf_op jit(solution)/shard_map/while/body/eval_jaxpr/reduce_sum | solution.py:40
  217.6 14.9 %fusion.80 = f32[2,16,256,128]{3,2,1,0:T(8,128)} fusion(f32[2,16,256,128]{3,2,1,0:T(8,128)} %get-tuple-element.297, f32[2,16,256]{2,1,0:T(8,128)S(1)} %get-tuple-element.281, pred[]{:T(512)S(6)} %compare.19, f32[2,768,256,16]{2,1,3,0:T(8,128)} %get-tuple-element.279, f32[2,16,256]{2,1,0:T(8,128)S(1)} %select_maximum_fusion.2, ...), kind=kOutput, calls=%fused_computation.12.clone.1 | convolution fusion | flops 1645215744 | bytes 34406400 | tf_op jit(solution)/shard_map/while/body/eval_jaxpr/rhqk,rkd->rhqd/dot_general | solution.py:41
  234.6 1.2 dynamic-slice_bitcast_fusion.2
  235.8 10.2 %fusion.77 = (f32[2,16,256]{2,1,0:T(8,128)S(1)}, f32[2,768,256,16]{2,1,3,0:T(8,128)}) fusion(pred[2,256,768]{1,2,0:T(8,128)(4,1)S(1)} %broadcast_select_fusion.2, bf16[2,256,16,128]{3,1,2,0:T(8,128)(2,1)S(1)} %get-tuple-element.313, bf16[2,768,256]{2,1,0:T(8,128)(2,1)S(1)} %dynamic-slice_bitcast_fusion.2), kind=kOutput, calls=%fused_computation.6.clone.1 | convolution fusion | flops 1629478912 | bytes 28082176 | tf_op jit(solution)/shard_map/while/body/eval_jaxpr/rqhd,rkd->rhqk/dot_general | solution.py:28
  246.1 11.4 %fusion.78 = f32[2,16,256]{2,1,0:T(8,128)S(1)} fusion(f32[2,768,256,16]{2,1,3,0:T(8,128)} %get-tuple-element.279, f32[2,16,256]{2,1,0:T(8,128)S(1)} %select_maximum_fusion.2, pred[2,256,768]{1,2,0:T(8,128)(4,1)S(1)} %broadcast_select_fusion.2), kind=kLoop, calls=%fused_computation.8.clone.1 | loop fusion | flops 31449088 | bytes 25624576 | tf_op jit(solution)/shard_map/while/body/eval_jaxpr/reduce_sum | solution.py:40
  257.5 14.9 %fusion.80 = f32[2,16,256,128]{3,2,1,0:T(8,128)} fusion(f32[2,16,256,128]{3,2,1,0:T(8,128)} %get-tuple-element.297, f32[2,16,256]{2,1,0:T(8,128)S(1)} %get-tuple-element.281, pred[]{:T(512)S(6)} %compare.19, f32[2,768,256,16]{2,1,3,0:T(8,128)} %get-tuple-element.279, f32[2,16,256]{2,1,0:T(8,128)S(1)} %select_maximum_fusion.2, ...), kind=kOutput, calls=%fused_computation.12.clone.1 | convolution fusion | flops 1645215744 | bytes 34406400 | tf_op jit(solution)/shard_map/while/body/eval_jaxpr/rhqk,rkd->rhqd/dot_general | solution.py:41
  274.6 1.2 dynamic-slice_bitcast_fusion.2
  275.8 10.2 %fusion.77 = (f32[2,16,256]{2,1,0:T(8,128)S(1)}, f32[2,768,256,16]{2,1,3,0:T(8,128)}) fusion(pred[2,256,768]{1,2,0:T(8,128)(4,1)S(1)} %broadcast_select_fusion.2, bf16[2,256,16,128]{3,1,2,0:T(8,128)(2,1)S(1)} %get-tuple-element.313, bf16[2,768,256]{2,1,0:T(8,128)(2,1)S(1)} %dynamic-slice_bitcast_fusion.2), kind=kOutput, calls=%fused_computation.6.clone.1 | convolution fusion | flops 1629478912 | bytes 28082176 | tf_op jit(solution)/shard_map/while/body/eval_jaxpr/rqhd,rkd->rhqk/dot_general | solution.py:28
  286.0 11.4 %fusion.78 = f32[2,16,256]{2,1,0:T(8,128)S(1)} fusion(f32[2,768,256,16]{2,1,3,0:T(8,128)} %get-tuple-element.279, f32[2,16,256]{2,1,0:T(8,128)S(1)} %select_maximum_fusion.2, pred[2,256,768]{1,2,0:T(8,128)(4,1)S(1)} %broadcast_select_fusion.2), kind=kLoop, calls=%fused_computation.8.clone.1 | loop fusion | flops 31449088 | bytes 25624576 | tf_op jit(solution)/shard_map/while/body/eval_jaxpr/reduce_sum | solution.py:40
  297.5 14.9 %fusion.80 = f32[2,16,256,128]{3,2,1,0:T(8,128)} fusion(f32[2,16,256,128]{3,2,1,0:T(8,128)} %get-tuple-element.297, f32[2,16,256]{2,1,0:T(8,128)S(1)} %get-tuple-element.281, pred[]{:T(512)S(6)} %compare.19, f32[2,768,256,16]{2,1,3,0:T(8,128)} %get-tuple-element.279, f32[2,16,256]{2,1,0:T(8,128)S(1)} %select_maximum_fusion.2, ...), kind=kOutput, calls=%fused_computation.12.clone.1 | convolution fusion | flops 1645215744 | bytes 34406400 | tf_op jit(solution)/shard_map/while/body/eval_jaxpr/rhqk,rkd->rhqd/dot_general | solution.py:41
  314.5 1.2 dynamic-slice_bitcast_fusion.2
  315.7 10.2 %fusion.77 = (f32[2,16,256]{2,1,0:T(8,128)S(1)}, f32[2,768,256,16]{2,1,3,0:T(8,128)}) fusion(pred[2,256,768]{1,2,0:T(8,128)(4,1)S(1)} %broadcast_select_fusion.2, bf16[2,256,16,128]{3,1,2,0:T(8,128)(2,1)S(1)} %get-tuple-element.313, bf16[2,768,256]{2,1,0:T(8,128)(2,1)S(1)} %dynamic-slice_bitcast_fusion.2), kind=kOutput, calls=%fused_computation.6.clone.1 | convolution fusion | flops 1629478912 | bytes 28082176 | tf_op jit(solution)/shard_map/while/body/eval_jaxpr/rqhd,rkd->rhqk/dot_general | solution.py:28
  326.0 11.4 %fusion.78 = f32[2,16,256]{2,1,0:T(8,128)S(1)} fusion(f32[2,768,256,16]{2,1,3,0:T(8,128)} %get-tuple-element.279, f32[2,16,256]{2,1,0:T(8,128)S(1)} %select_maximum_fusion.2, pred[2,256,768]{1,2,0:T(8,128)(4,1)S(1)} %broadcast_select_fusion.2), kind=kLoop, calls=%fused_computation.8.clone.1 | loop fusion | flops 31449088 | bytes 25624576 | tf_op jit(solution)/shard_map/while/body/eval_jaxpr/reduce_sum | solution.py:40
  337.4 14.9 %fusion.80 = f32[2,16,256,128]{3,2,1,0:T(8,128)} fusion(f32[2,16,256,128]{3,2,1,0:T(8,128)} %get-tuple-element.297, f32[2,16,256]{2,1,0:T(8,128)S(1)} %get-tuple-element.281, pred[]{:T(512)S(6)} %compare.19, f32[2,768,256,16]{2,1,3,0:T(8,128)} %get-tuple-element.279, f32[2,16,256]{2,1,0:T(8,128)S(1)} %select_maximum_fusion.2, ...), kind=kOutput, calls=%fused_computation.12.clone.1 | convolution fusion | flops 1645215744 | bytes 34406400 | tf_op jit(solution)/shard_map/while/body/eval_jaxpr/rhqk,rkd->rhqd/dot_general | solution.py:41
  354.5 1.2 dynamic-slice_bitcast_fusion.2
  355.7 10.2 %fusion.77 = (f32[2,16,256]{2,1,0:T(8,128)S(1)}, f32[2,768,256,16]{2,1,3,0:T(8,128)}) fusion(pred[2,256,768]{1,2,0:T(8,128)(4,1)S(1)} %broadcast_select_fusion.2, bf16[2,256,16,128]{3,1,2,0:T(8,128)(2,1)S(1)} %get-tuple-element.313, bf16[2,768,256]{2,1,0:T(8,128)(2,1)S(1)} %dynamic-slice_bitcast_fusion.2), kind=kOutput, calls=%fused_computation.6.clone.1 | convolution fusion | flops 1629478912 | bytes 28082176 | tf_op jit(solution)/shard_map/while/body/eval_jaxpr/rqhd,rkd->rhqk/dot_general | solution.py:28
  365.9 11.4 %fusion.78 = f32[2,16,256]{2,1,0:T(8,128)S(1)} fusion(f32[2,768,256,16]{2,1,3,0:T(8,128)} %get-tuple-element.279, f32[2,16,256]{2,1,0:T(8,128)S(1)} %select_maximum_fusion.2, pred[2,256,768]{1,2,0:T(8,128)(4,1)S(1)} %broadcast_select_fusion.2), kind=kLoop, calls=%fused_computation.8.clone.1 | loop fusion | flops 31449088 | bytes 25624576 | tf_op jit(solution)/shard_map/while/body/eval_jaxpr/reduce_sum | solution.py:40
  377.4 14.9 %fusion.80 = f32[2,16,256,128]{3,2,1,0:T(8,128)} fusion(f32[2,16,256,128]{3,2,1,0:T(8,128)} %get-tuple-element.297, f32[2,16,256]{2,1,0:T(8,128)S(1)} %get-tuple-element.281, pred[]{:T(512)S(6)} %compare.19, f32[2,768,256,16]{2,1,3,0:T(8,128)} %get-tuple-element.279, f32[2,16,256]{2,1,0:T(8,128)S(1)} %select_maximum_fusion.2, ...), kind=kOutput, calls=%fused_computation.12.clone.1 | convolution fusion | flops 1645215744 | bytes 34406400 | tf_op jit(solution)/shard_map/while/body/eval_jaxpr/rhqk,rkd->rhqd/dot_general | solution.py:41
  395.6 10.2 %fusion.77 = (f32[2,16,256]{2,1,0:T(8,128)S(1)}, f32[2,768,256,16]{2,1,3,0:T(8,128)}) fusion(pred[2,256,768]{1,2,0:T(8,128)(4,1)S(1)} %broadcast_select_fusion.2, bf16[2,256,16,128]{3,1,2,0:T(8,128)(2,1)S(1)} %get-tuple-element.313, bf16[2,768,256]{2,1,0:T(8,128)(2,1)S(1)} %dynamic-slice_bitcast_fusion.2), kind=kOutput, calls=%fused_computation.6.clone.1 | convolution fusion | flops 1629478912 | bytes 28082176 | tf_op jit(solution)/shard_map/while/body/eval_jaxpr/rqhd,rkd->rhqk/dot_general | solution.py:28
  405.9 11.4 %fusion.78 = f32[2,16,256]{2,1,0:T(8,128)S(1)} fusion(f32[2,768,256,16]{2,1,3,0:T(8,128)} %get-tuple-element.279, f32[2,16,256]{2,1,0:T(8,128)S(1)} %select_maximum_fusion.2, pred[2,256,768]{1,2,0:T(8,128)(4,1)S(1)} %broadcast_select_fusion.2), kind=kLoop, calls=%fused_computation.8.clone.1 | loop fusion | flops 31449088 | bytes 25624576 | tf_op jit(solution)/shard_map/while/body/eval_jaxpr/reduce_sum | solution.py:40
  417.3 14.9 %fusion.80 = f32[2,16,256,128]{3,2,1,0:T(8,128)} fusion(f32[2,16,256,128]{3,2,1,0:T(8,128)} %get-tuple-element.297, f32[2,16,256]{2,1,0:T(8,128)S(1)} %get-tuple-element.281, pred[]{:T(512)S(6)} %compare.19, f32[2,768,256,16]{2,1,3,0:T(8,128)} %get-tuple-element.279, f32[2,16,256]{2,1,0:T(8,128)S(1)} %select_maximum_fusion.2, ...), kind=kOutput, calls=%fused_computation.12.clone.1 | convolution fusion | flops 1645215744 | bytes 34406400 | tf_op jit(solution)/shard_map/while/body/eval_jaxpr/rhqk,rkd->rhqd/dot_general | solution.py:41
  434.4 1.2 dynamic-slice_bitcast_fusion.2
  435.6 10.2 %fusion.77 = (f32[2,16,256]{2,1,0:T(8,128)S(1)}, f32[2,768,256,16]{2,1,3,0:T(8,128)}) fusion(pred[2,256,768]{1,2,0:T(8,128)(4,1)S(1)} %broadcast_select_fusion.2, bf16[2,256,16,128]{3,1,2,0:T(8,128)(2,1)S(1)} %get-tuple-element.313, bf16[2,768,256]{2,1,0:T(8,128)(2,1)S(1)} %dynamic-slice_bitcast_fusion.2), kind=kOutput, calls=%fused_computation.6.clone.1 | convolution fusion | flops 1629478912 | bytes 28082176 | tf_op jit(solution)/shard_map/while/body/eval_jaxpr/rqhd,rkd->rhqk/dot_general | solution.py:28
  445.8 11.4 %fusion.78 = f32[2,16,256]{2,1,0:T(8,128)S(1)} fusion(f32[2,768,256,16]{2,1,3,0:T(8,128)} %get-tuple-element.279, f32[2,16,256]{2,1,0:T(8,128)S(1)} %select_maximum_fusion.2, pred[2,256,768]{1,2,0:T(8,128)(4,1)S(1)} %broadcast_select_fusion.2), kind=kLoop, calls=%fused_computation.8.clone.1 | loop fusion | flops 31449088 | bytes 25624576 | tf_op jit(solution)/shard_map/while/body/eval_jaxpr/reduce_sum | solution.py:40
  457.3 14.9 %fusion.80 = f32[2,16,256,128]{3,2,1,0:T(8,128)} fusion(f32[2,16,256,128]{3,2,1,0:T(8,128)} %get-tuple-element.297, f32[2,16,256]{2,1,0:T(8,128)S(1)} %get-tuple-element.281, pred[]{:T(512)S(6)} %compare.19, f32[2,768,256,16]{2,1,3,0:T(8,128)} %get-tuple-element.279, f32[2,16,256]{2,1,0:T(8,128)S(1)} %select_maximum_fusion.2, ...), kind=kOutput, calls=%fused_computation.12.clone.1 | convolution fusion | flops 1645215744 | bytes 34406400 | tf_op jit(solution)/shard_map/while/body/eval_jaxpr/rhqk,rkd->rhqd/dot_general | solution.py:41
  472.2 2.9 fusion.39
  475.0 1.4 copy.38
  476.4 2.3 stack_reshape.6
  478.7 2.6 pad_maximum_fusion
  481.3 6.3 copy.39
  487.6 4.1 broadcast_in_dim.112
  491.7 64.2 %scatter_fusion = bf16[512,2,2048]{2,1,0:T(2,128)(2,1)} fusion(bf16[512,2,2048]{2,1,0:T(2,128)(2,1)} %broadcast_in_dim.112, s32[512]{0:T(512)S(1)} %bitcast.107, bf16[512,2,2048]{2,1,0:T(2,128)(2,1)} %copy.39), kind=kCustom, calls=%fused_computation.1 | custom fusion | bytes 12584960 | tf_op jit(solution)/shard_map/scatter | solution.py:151
  555.9 3.6 all-to-all-start.1
  560.1 1.4 reduce.5
  561.6 93.9 %all-to-all-done.1 = bf16[32,16,2,2048]{3,2,1,0:T(2,128)(2,1)} async-done(((bf16[32,16,2,2048]{3,2,1,0:T(2,128)(2,1)}), bf16[32,16,2,2048]{3,2,1,0:T(2,128)(2,1)}, u32[]{:S(2)}, u32[]{:S(2)}) %all-to-all-start.1) | async-done | bytes 4194336 | tf_op jit(solution)/shard_map/all_to_all | solution.py:154
  656.0 43.0 %scatter_fusion.1 = bf16[128,2,2048]{2,1,0:T(2,128)(2,1)S(1)} fusion(bf16[128,2,2048]{2,1,0:T(2,128)(2,1)S(1)} %broadcast_in_dim.106, s32[512]{0:T(512)S(1)} %bitcast.108, bf16[512,2,2048]{2,1,0:T(2,128)(2,1)} %bitcast.11), kind=kCustom, calls=%fused_computation.2 | custom fusion | bytes 12584960 | tf_op jit(solution)/shard_map/scatter | solution.py:173
  699.1 1.5 fusion.60
  700.6 5.5 fusion.61
  707.5 70.8 %all-gather.2.cloned.1.call-done = bf16[1024,2048]{1,0:T(8,128)(2,1)} async-done(((bf16[128,2048]{1,0:T(8,128)(2,1)}), bf16[1024,2048]{1,0:T(8,128)(2,1)}) %all-gather.2.cloned.1.call-update) | async-done | bytes 4194320 | tf_op jit(solution)/shard_map/all_gather | solution.py:183
  778.2 15.3 %convolution_convert_fusion = bf16[1024,2048]{1,0:T(8,128)(2,1)} fusion(bf16[1024,2048]{1,0:T(8,128)(2,1)} %param.28, f32[1024]{0:T(1024)S(1)} %copy-done.11, bf16[1024,2048]{1,0:T(8,128)(2,1)} %all-gather.2.cloned.1.call-done, bf16[2048,1024]{1,0:T(8,128)(2,1)} %param.26), kind=kOutput, calls=%fused_computation.51 | convolution fusion | flops 8602517504 | bytes 16781312 | tf_op jit(solution)/shard_map/dot_general | solution.py:190
  793.5 86.3 %reduce-scatter.2.cloned.1.call-done = bf16[128,2048]{1,0:T(8,128)(2,1)} async-done(((bf16[1024,2048]{1,0:T(8,128)(2,1)}), bf16[128,2048]{1,0:T(8,128)(2,1)}) %reduce-scatter.2.cloned.1.call-update) | async-done | bytes 524304 | tf_op jit(solution)/shard_map/reduce_scatter | solution.py:191
  879.8 2.0 add_convert_fusion
  (162 shorter events, 36.9 us)
Async XLA Ops:
  6.5 123.5 %copy-start = (bf16[2,512,256]{2,1,0:T(8,128)(2,1)S(1)}, bf16[2,512,256]{2,1,0:T(8,128)(2,1)}, u32[]{:S(2)}) copy-start(bf16[2,512,256]{2,1,0:T(8,128)(2,1)} %param.18) | copy-start | bytes 1572868
  6.5 114.2 %copy-start.12 = (s32[8]{0:T(128)S(1)}, s32[8]{0:T(128)}, u32[]{:S(2)}) copy-start(s32[8]{0:T(128)} %param.20) | copy-start | bytes 100
  7.7 122.4 %copy-start.4 = (bf16[2,256,256]{2,1,0:T(8,128)(2,1)S(1)}, bf16[2,256,256]{2,1,0:T(8,128)(2,1)}, u32[]{:S(2)}) copy-start(bf16[2,256,256]{2,1,0:T(8,128)(2,1)} %param.17) | copy-start | bytes 786436
  8.7 23.6 %collective-permute-start = (bf16[2,768,256]{2,1,0:T(8,128)(2,1)S(1)}, bf16[2,768,256]{2,1,0:T(8,128)(2,1)S(1)}, u32[]{:S(2)}, u32[]{:S(2)}) collective-permute-start(bf16[2,768,256]{2,1,0:T(8,128)(2,1)S(1)} %constant_dynamic-update-slice_fusion), channel_id=1, source_target_pairs={{0,1},{1,2},{2,3},{3,4},{4,5},{5,6},{6,7},{7,0},{8,9},{9,10},{10,1... | collective-permute-start | bytes 2359304 | tf_op jit(solution)/shard_map/ppermute | solution.py:115
  32.3 0.9 copy-start.1
  33.2 33.4 %collective-permute-start.1 = (bf16[2,768,256]{2,1,0:T(8,128)(2,1)S(1)}, bf16[2,768,256]{2,1,0:T(8,128)(2,1)S(1)}, u32[]{:S(2)}, u32[]{:S(2)}) collective-permute-start(bf16[2,768,256]{2,1,0:T(8,128)(2,1)S(1)} %collective-permute-done), channel_id=1, source_target_pairs={{0,1},{1,2},{2,3},{3,4},{4,5},{5,6},{6,7},{7,0},{8,9},{9,10},{10,1... | collective-permute-start | bytes 2359304 | tf_op jit(solution)/shard_map/ppermute | solution.py:115
  33.2 36.6 %collective-permute-start.4 = (bf16[2,768,256]{2,1,0:T(8,128)(2,1)S(1)}, bf16[2,768,256]{2,1,0:T(8,128)(2,1)}, u32[]{:S(2)}, u32[]{:S(2)}) collective-permute-start(bf16[2,768,256]{2,1,0:T(8,128)(2,1)S(1)} %constant_dynamic-update-slice_fusion), channel_id=1, source_target_pairs={{0,7},{1,0},{2,1},{3,2},{4,3},{5,4},{6,5},{7,6},{8,15},{9,8},{10,9... | collective-permute-start | bytes 2359304 | tf_op jit(solution)/shard_map/ppermute | solution.py:117
  66.6 51.0 %copy-start.3 = (bf16[2,768,256]{2,1,0:T(8,128)(2,1)}, bf16[2,768,256]{2,1,0:T(8,128)(2,1)S(1)}, u32[]{:S(2)}) copy-start(bf16[2,768,256]{2,1,0:T(8,128)(2,1)S(1)} %collective-permute-done.1) | copy-start | bytes 2359300
  66.6 35.1 %collective-permute-start.2 = (bf16[2,768,256]{2,1,0:T(8,128)(2,1)S(1)}, bf16[2,768,256]{2,1,0:T(8,128)(2,1)}, u32[]{:S(2)}, u32[]{:S(2)}) collective-permute-start(bf16[2,768,256]{2,1,0:T(8,128)(2,1)S(1)} %collective-permute-done.1), channel_id=1, source_target_pairs={{0,1},{1,2},{2,3},{3,4},{4,5},{5,6},{6,7},{7,0},{8,9},{9,10},{10,1... | collective-permute-start | bytes 2359304 | tf_op jit(solution)/shard_map/ppermute | solution.py:115
  69.8 51.0 %collective-permute-start.5 = (bf16[2,768,256]{2,1,0:T(8,128)(2,1)}, bf16[2,768,256]{2,1,0:T(8,128)(2,1)}, u32[]{:S(2)}, u32[]{:S(2)}) collective-permute-start(bf16[2,768,256]{2,1,0:T(8,128)(2,1)} %collective-permute-done.4), channel_id=1, source_target_pairs={{0,7},{1,0},{2,1},{3,2},{4,3},{5,4},{6,5},{7,6},{8,15},{9,8},{10,9... | collective-permute-start | bytes 2359304 | tf_op jit(solution)/shard_map/ppermute | solution.py:117
  101.8 23.6 %collective-permute-start.3 = (bf16[2,768,256]{2,1,0:T(8,128)(2,1)}, bf16[2,768,256]{2,1,0:T(8,128)(2,1)}, u32[]{:S(2)}, u32[]{:S(2)}) collective-permute-start(bf16[2,768,256]{2,1,0:T(8,128)(2,1)} %collective-permute-done.2), channel_id=1, source_target_pairs={{0,1},{1,2},{2,3},{3,4},{4,5},{5,6},{6,7},{7,0},{8,9},{9,10},{10,1... | collective-permute-start | bytes 2359304 | tf_op jit(solution)/shard_map/ppermute | solution.py:115
  107.3 10.4 %copy-start.9 = (s32[512,1]{0,1:T(1,128)}, s32[512,1]{0,1:T(1,128)S(1)}, u32[]{:S(2)}) copy-start(s32[512,1]{0,1:T(1,128)S(1)} %compare_select_fusion.2) | copy-start | bytes 6148
  110.4 445.5 %all-to-all-start = ((s32[32,1,16]{2,1,0:T(1,128)}), s32[32,1,16]{2,1,0:T(1,128)}, u32[]{:S(2)}, u32[]{:S(2)}) async-start(s32[32,1,16]{2,1,0:T(1,128)} %bitcast.3), calls=%async_computation | async-start | bytes 32768 | tf_op jit(solution)/shard_map/all_to_all | solution.py:161
  120.8 25.5 %copy-start.2 = (bf16[2,768,256]{2,1,0:T(8,128)(2,1)S(1)}, bf16[2,768,256]{2,1,0:T(8,128)(2,1)}, u32[]{:S(2)}) copy-start(bf16[2,768,256]{2,1,0:T(8,128)(2,1)} %copy-done.1) | copy-start | bytes 2359300
  120.8 21.9 %collective-permute-start.6 = (bf16[2,768,256]{2,1,0:T(8,128)(2,1)}, bf16[2,768,256]{2,1,0:T(8,128)(2,1)S(1)}, u32[]{:S(2)}, u32[]{:S(2)}) collective-permute-start(bf16[2,768,256]{2,1,0:T(8,128)(2,1)} %collective-permute-done.5), channel_id=1, source_target_pairs={{0,7},{1,0},{2,1},{3,2},{4,3},{5,4},{6,5},{7,6},{8,15},{9,8},{10,9... | collective-permute-start | bytes 2359304 | tf_op jit(solution)/shard_map/ppermute | solution.py:117
  481.3 10.4 %copy-start.10 = (s32[512,1]{0,1:T(1,128)S(1)}, s32[512,1]{0,1:T(1,128)}, u32[]{:S(2)}) copy-start(s32[512,1]{0,1:T(1,128)} %copy-done.9) | copy-start | bytes 6148
  555.9 99.5 %all-to-all-start.1 = ((bf16[32,16,2,2048]{3,2,1,0:T(2,128)(2,1)}), bf16[32,16,2,2048]{3,2,1,0:T(2,128)(2,1)}, u32[]{:S(2)}, u32[]{:S(2)}) async-start(bf16[32,16,2,2048]{3,2,1,0:T(2,128)(2,1)} %bitcast.97), calls=%async_computation.1 | async-start | bytes 8388608 | tf_op jit(solution)/shard_map/all_to_all | solution.py:154
  559.5 218.7 %all-gather.2.cloned.1.call-start = ((), (), s32[]{:S(2)}) async-start(), calls=%async_computation.3 | async-start | bytes 4718592 | tf_op jit(solution)/shard_map/all_gather | solution.py:183
  656.0 44.6 %copy-start.5 = (f32[2048]{0:T(1024)S(1)}, f32[2048]{0:T(1024)}, u32[]{:S(2)}) copy-start(f32[2048]{0:T(1024)} %param.23) | copy-start | bytes 24580
  700.6 5.8 copy-start.6
  700.6 5.8 copy-start.7
  700.6 77.7 %copy-start.11 = (f32[1024]{0:T(1024)S(1)}, f32[1024]{0:T(1024)}, u32[]{:S(2)}) copy-start(f32[1024]{0:T(1024)} %param.27) | copy-start | bytes 12292
  707.4 172.4 %copy-start.8 = (f32[2048]{0:T(1024)S(1)}, f32[2048]{0:T(1024)}, u32[]{:S(2)}) copy-start(f32[2048]{0:T(1024)} %param.29) | copy-start | bytes 24580
  707.4 172.4 %reduce-scatter.2.cloned.1.call-start = ((), (), s32[]{:S(2)}) async-start(), calls=%async_computation.4 | async-start | bytes 4718592 | tf_op jit(solution)/shard_map/reduce_scatter | solution.py:191
Sparse Core Ops, SparseCore 0:
  707.5 70.6 all-gather.1
  793.6 86.1 reduce-scatter.1
